TPU v7x, 32 devices: a whole 2x2x4 slice. The times are simulated.
32 devices in a mesh: expert: 8 (over z, x), tensor: 4 (over y, core).
Axes of the slice: x: 2, y: 2, z: 4, core: 2. Of those that a mesh axis runs over, the one named last changes fastest.
Arguments:
- context: bfloat16 [2048, 2048], P('expert', 'tensor'), may hold values from -0.25976562 to 0.25976562
- out_proj: bfloat16 [2048, 2048], P('tensor'), may hold values from -0.125 to 0.125
- residual: bfloat16 [2048, 2048], P(('expert', 'tensor')), may hold values from -0.25976562 to 0.25976562
- norm_gain: float32 [2048], replicated, may hold values from 0.1 to 1.9
- router_weight: float32 [2048, 64], replicated, may hold values from -5.524272 to 5.524272
- expert_ids: int32 [2048, 8], P('expert'), may hold values from 0 to 63, all different within a row; in each aligned block of 64 rows (0 to 63, 64 to 127, ...) at most 10 rows name the same one
- placement: int32 [128], replicated, may hold values from 0 to 63, as said below
- expert_weights: bfloat16 [128, 3, 2048, 1024], P('expert', None, None, 'tensor'), as said below
- post_gain: float32 [2048], replicated, may hold values from 0.5 to 1.5
Outputs:
- hidden_out: float32 [2048, 2048], P(('expert', 'tensor'))
- normed_out: float32 [2048, 2048], P(('expert', 'tensor'))
Inputs may be any that keep to these rules, and one draw needn't show every extreme that they name: `expert_ids`: each row names 8 different experts. In each aligned block of 64 rows (the rows of one device) no expert is named by more than 10 rows, a bound that some block reaches; every expert is named somewhere. `placement`: every expert is held by one, three or five slots. `expert_weights`: slots that hold the same expert carry equal weights.
All inputs are finite; a program needn't handle non-finite values.
Results may differ from a plain program's by a relative error of at most 0.018.
Values may be sent and summed in bfloat16 or wider, within the bound.
No kernel may reach another device: no remote copies, remote signals or barrier semaphores. Data moves between devices by JAX's collectives and lax.ppermute only.
A program may use at most 256 MiB of HBM per device.

v0:
```python
import jax
import jax.numpy as jnp
from jax import lax
from jax.sharding import PartitionSpec as P

EPS = 1e-06


def rms_scale(values, gain_row):
    mean_square = jnp.mean(values * values, axis=-1, keepdims=True)
    return values * lax.rsqrt(mean_square + EPS) * gain_row


def expert_inner(block_rows, weights):
    both_pre = jnp.einsum(
        "nqsmd,scdf->nqsmcf", block_rows, weights[:, :2], preferred_element_type=jnp.float32
    )
    return jax.nn.silu(both_pre[..., 0, :]) * both_pre[..., 1, :]


def expert_down(inner_act, weights):
    return jnp.einsum(
        "nqsmf,sdf->nqsmd", inner_act, weights[:, 2], preferred_element_type=jnp.float32
    )


def on_device(
    context,
    out_proj,
    residual,
    norm_gain,
    router_weight,
    expert_ids,
    placement,
    expert_weights,
    post_gain,
):
    groups = lax.axis_size("tensor")
    holders = lax.axis_size("expert")
    my_group = lax.axis_index("tensor")
    my_holder = lax.axis_index("expert")
    row_count = residual.shape[0]
    model_width = residual.shape[1]
    top_count = expert_ids.shape[1]
    expert_count = router_weight.shape[1]
    slot_dev = expert_weights.shape[0]
    slot_total = placement.shape[0]
    blocks = holders * groups
    capacity = max(2, row_count * top_count * 5 // (expert_count * 4))
    expert_range = jnp.arange(expert_count, dtype=jnp.int32)
    slot_range = jnp.arange(slot_total, dtype=jnp.int32)
    attention_parts = lax.all_to_all(
        jnp.dot(context, out_proj, preferred_element_type=jnp.float32)
        .astype(jnp.bfloat16)
        .reshape(groups, row_count, -1),
        "tensor",
        split_axis=0,
        concat_axis=0,
        tiled=True,
    )
    attention = jnp.sum(attention_parts.astype(jnp.float32), axis=0)
    hidden_mid = residual.astype(jnp.float32) + attention
    normed_full = rms_scale(hidden_mid, norm_gain)
    normed = normed_full.astype(jnp.bfloat16)
    logits = jnp.dot(normed_full, router_weight, precision=lax.Precision.HIGHEST)
    own_ids = lax.dynamic_slice_in_dim(expert_ids, my_group * row_count, row_count, 0)
    own_onehot = own_ids[:, :, None] == expert_range[None, None, :]
    chosen = jnp.sum(jnp.where(own_onehot, logits[:, None, :], 0.0), axis=-1)
    gate_weights = jax.nn.softmax(chosen, axis=-1)
    gate_hi = gate_weights.astype(jnp.bfloat16)
    gate_lo = (gate_weights - gate_hi.astype(jnp.float32)).astype(jnp.bfloat16)
    side = jnp.concatenate([own_ids.astype(jnp.bfloat16), gate_hi, gate_lo], axis=1)
    side = jnp.pad(side, ((0, 0), (0, 128 - 3 * top_count)))
    packed = lax.all_gather(
        jnp.concatenate([normed, side], axis=1), ("expert", "tensor"), axis=0, tiled=True
    ).reshape(blocks, row_count, model_width + 128)
    all_rows = packed[:, :, :model_width]
    all_ids = packed[:, :, model_width : model_width + top_count].astype(jnp.int32)
    all_hi = packed[:, :, model_width + top_count : model_width + 2 * top_count]
    all_lo = packed[:, :, model_width + 2 * top_count : model_width + 3 * top_count]
    holds = (placement[None, :] == expert_range[:, None]).astype(jnp.int32)
    copies = jnp.sum(holds, axis=1)
    copy_rank = jnp.cumsum(holds, axis=1) - 1
    holder_range = jnp.arange(holders, dtype=jnp.int32)
    copy_pick = holder_range[:, None] % copies[None, :]
    picked = (holds[None] > 0) & (copy_rank[None] == copy_pick[:, :, None])
    slot_pick = jnp.sum(jnp.where(picked, slot_range[None, None, :], 0), axis=2)
    local_range = jnp.arange(slot_dev, dtype=jnp.int32)
    mine_map = (slot_pick[:, :, None] == my_holder * slot_dev + local_range).astype(jnp.bfloat16)
    block_holder = jnp.arange(blocks, dtype=jnp.int32) // groups
    block_map = mine_map[block_holder]
    names = all_ids[:, :, :, None] == expert_range
    name_hot = jnp.any(names, axis=2).astype(jnp.bfloat16)
    gate_e_hi = jnp.sum(jnp.where(names, all_hi[:, :, :, None], 0), axis=2).astype(jnp.bfloat16)
    gate_e_lo = jnp.sum(jnp.where(names, all_lo[:, :, :, None], 0), axis=2).astype(jnp.bfloat16)
    stack = jnp.concatenate([name_hot, gate_e_hi, gate_e_lo], axis=1)
    per_slot = jnp.einsum("bue,bes->bus", stack, block_map, preferred_element_type=jnp.float32)
    token_hit = per_slot[:, :row_count]
    gate_sel_hi = per_slot[:, row_count : 2 * row_count]
    gate_sel_lo = per_slot[:, 2 * row_count :]
    token_range = jnp.arange(row_count, dtype=jnp.int32)
    earlier = (token_range[None, :] < token_range[:, None]).astype(jnp.bfloat16)
    count_before = jnp.einsum(
        "uv,bvs->bus", earlier, token_hit.astype(jnp.bfloat16), preferred_element_type=jnp.float32
    )
    rank_range = jnp.arange(capacity, dtype=jnp.float32)
    pick = token_hit[..., None] * (count_before[..., None] == rank_range)
    pick_hot = pick.astype(jnp.bfloat16)
    received = (
        jnp.einsum("busr,bud->bsrd", pick_hot, all_rows, preferred_element_type=jnp.float32)
        .astype(jnp.bfloat16)
        .reshape(holders, groups, slot_dev, capacity, model_width)
    )
    inner_f32 = expert_inner(received, expert_weights)
    if blocks * row_count * model_width * 4 <= 32 << 20:
        gate_sel = gate_sel_hi + gate_sel_lo
        pair_gate = jnp.sum(pick * gate_sel[..., None], axis=1)
        pair_gate = pair_gate.reshape(holders, groups, slot_dev, capacity, 1)
        inner_act = (inner_f32 * pair_gate).astype(jnp.bfloat16)
        partial_value = expert_down(inner_act, expert_weights).astype(jnp.bfloat16)
        partial_value = partial_value.reshape(blocks, slot_dev, capacity, model_width)
        combined = jnp.einsum(
            "hqusr,hqsrd->qhud",
            pick_hot.reshape(holders, groups, row_count, slot_dev, capacity),
            partial_value.reshape(holders, groups, slot_dev, capacity, model_width),
            preferred_element_type=jnp.float32,
        )
        moe_sum = lax.psum_scatter(
            combined.astype(jnp.bfloat16).reshape(-1, model_width),
            "tensor",
            scatter_dimension=0,
            tiled=True,
        ).reshape(holders, row_count, model_width)
        moe_sum = lax.all_to_all(moe_sum, "expert", split_axis=0, concat_axis=0, tiled=True)
        moe_sum = jnp.sum(moe_sum.astype(jnp.float32), axis=0)
    else:
        partial_value = expert_down(inner_f32.astype(jnp.bfloat16), expert_weights).astype(
            jnp.bfloat16
        )
        expert_sum = lax.psum_scatter(partial_value, "tensor", scatter_dimension=1, tiled=True)
        returned = lax.all_to_all(expert_sum, "expert", split_axis=0, concat_axis=0, tiled=True)
        own_flat = own_ids.reshape(-1)
        own_onehot_flat = own_flat[:, None] == expert_range
        slot_of = jnp.sum(jnp.where(own_onehot_flat, slot_pick[my_holder][None, :], 0), axis=-1)
        slot_hot = (slot_of[:, None] == slot_range).astype(jnp.int32)
        rank_in = jnp.sum(jnp.cumsum(slot_hot, axis=0) * slot_hot, axis=-1) - 1
        own_index = slot_of * capacity + rank_in
        outputs = returned.reshape(-1, model_width)[own_index].reshape(
            row_count, top_count, model_width
        )
        moe_sum = jnp.einsum("rk,rkd->rd", gate_weights, outputs.astype(jnp.float32))
    hidden_out = hidden_mid + moe_sum
    normed_out = rms_scale(hidden_out, post_gain)
    return (hidden_out, normed_out)


def solution(mesh):
    in_specs = (
        P("expert", "tensor"),
        P("tensor", None),
        P(("expert", "tensor"), None),
        P(),
        P(),
        P("expert", None),
        P(),
        P("expert", None, None, "tensor"),
        P(),
    )
    out_specs = (P(("expert", "tensor"), None), P(("expert", "tensor"), None))
    return jax.shard_map(
        on_device, mesh=mesh, in_specs=in_specs, out_specs=out_specs, check_vma=False
    )
```

profile of v0, /device:TPU:0, one launch (start us, length us, event | category | flops | bytes accessed | tf_op | source)
XLA Modules:
  0.0 380.9 jit_solution(10148748740071930744)
XLA Ops:
  7.2 1.5 copy-done
  8.8 2.7 convolution_convert_fusion.1
  11.4 4.2 %all-to-all-start = ((bf16[4,64,2048]{2,1,0:T(8,128)(2,1)}), bf16[4,64,2048]{2,1,0:T(8,128)(2,1)S(1)}, u32[]{:S(2)}, u32[]{:S(2)}) async-start(bf16[4,64,2048]{2,1,0:T(8,128)(2,1)} %bitcast), calls=%async_computation | async-start | bytes 2097152 | tf_op jit(solution)/shard_map/all_to_all | solution.py:52
  15.7 0.8 fusion.66
  16.5 13.6 %all-to-all-done = bf16[4,64,2048]{2,1,0:T(8,128)(2,1)S(1)} async-done(((bf16[4,64,2048]{2,1,0:T(8,128)(2,1)}), bf16[4,64,2048]{2,1,0:T(8,128)(2,1)S(1)}, u32[]{:S(2)}, u32[]{:S(2)}) %all-to-all-start) | async-done | bytes 1048608 | tf_op jit(solution)/shard_map/all_to_all | solution.py:52
  30.3 1.1 multiply_reduce_fusion.1
  31.4 1.1 fusion.41
  36.2 79.1 %all-gather.2.cloned.1.call-done = bf16[2048,2176]{1,0:T(8,128)(2,1)} async-done(((bf16[64,2176]{1,0:T(8,128)(2,1)}), bf16[2048,2176]{1,0:T(8,128)(2,1)}) %all-gather.2.cloned.1.call-update) | async-done | bytes 8912912 | tf_op jit(solution)/shard_map/all_gather | solution.py:74
  115.3 2.1 fusion.67
  117.5 3.5 fusion.18
  121.0 1.0 copy.55
  122.1 8.8 %fusion.21 = (bf16[32,64,64]{2,1,0:T(8,128)(2,1)}, bf16[32,64,64]{2,1,0:T(8,128)(2,1)S(1)}) fusion(s32[32,64,8]{2,1,0:T(8,128)S(1)} %get-tuple-element.10, bf16[32,64,8]{2,1,0:T(8,128)(2,1)S(1)} %get-tuple-element.9, bf16[32,64,8]{2,1,0:T(8,128)(2,1)S(1)} %get-tuple-element.8), kind=kLoop, calls=%fused_computation.23 | loop fusion | flops 4980736 | bytes 655360 | tf_op jit(solution)/shard_map/reduce_sum | solution.py:94
  130.9 1.3 copy.56
  132.2 1.1 convert_element_type.89
  133.3 1.0 copy.57
  134.3 1.7 fusion.33
  136.5 13.4 %convolution_convert_fusion = bf16[32,16,10,2048]{3,1,2,0:T(8,128)(2,1)} fusion(bf16[32,64,2176]{2,1,0:T(8,128)(2,1)} %bitcast.79, f32[32,64,16]{1,2,0:T(8,128)S(1)} %get-tuple-element.12, f32[32,64,16]{1,2,0:T(8,128)S(1)} %copy.61), kind=kOutput, calls=%fused_computation.11 | convolution fusion | flops 1353318400 | bytes 29622272 | tf_op jit(solution)/shard_map/busr,bud->bsrd/dot_general | solution.py:110
  149.9 0.8 fusion.26
  151.2 46.3 %fusion.8 = f32[8,4,16,10,2,256]{5,3,4,1,0,2:T(8,128)} fusion(bf16[16,3,2048,256]{3,2,1,0:T(8,128)(2,1)} %param.16, bf16[8,4,16,10,2048,1]{4,2,3,1,0,5:T(8,128)(2,1)} %bitcast.76), kind=kOutput, calls=%fused_computation.12 | convolution fusion | flops 10737418240 | bytes 65011712 | tf_op jit(solution)/shard_map/nqsmd,scdf->nqsmcf/dot_general | solution.py:15
  197.5 23.3 %convert_bitcast_fusion = bf16[8,4,16,10,2048]{4,3,1,0,2:T(8,128)(2,1)} fusion(bf16[16,3,2048,256]{3,2,1,0:T(8,128)(2,1)} %param.16, f32[8,4,16,10,2,256]{5,3,4,1,0,2:T(8,128)} %fusion.8, f32[8,4,16,10]{3,1,0,2:T(4,128)S(1)} %copy.64), kind=kOutput, calls=%fused_computation.4 | convolution fusion | flops 5388369920 | bytes 54546432 | tf_op jit(solution)/shard_map/nqsmf,sdf->nqsmd/dot_general | solution.py:22
  220.8 27.4 %bitcast_convert_fusion = bf16[4,8,64,2048]{3,2,1,0:T(8,128)(2,1)} fusion(bf16[8,4,16,10,2048]{4,3,1,0,2:T(8,128)(2,1)} %convert_bitcast_fusion, f32[8,4,64,16]{2,3,0,1:T(8,128)S(1)} %copy.59, f32[8,4,64,16]{2,3,1,0:T(8,128)S(1)} %bitcast.80), kind=kOutput, calls=%fused_computation.9 | convolution fusion | flops 1347026944 | bytes 29622272 | tf_op jit(solution)/shard_map/hqusr,hqsrd->qhud/dot_general | solution.py:122
  248.3 70.5 %reduce-scatter.2.cloned.1.call-done = bf16[512,2048]{1,0:T(8,128)(2,1)} async-done(((bf16[2048,2048]{1,0:T(8,128)(2,1)}), bf16[512,2048]{1,0:T(8,128)(2,1)}) %reduce-scatter.2.cloned.1.call-update) | async-done | bytes 2097168 | tf_op jit(solution)/shard_map/reduce_scatter | solution.py:128
  318.8 53.7 %all_to_all.10 = bf16[8,64,2048]{2,1,0:T(8,128)(2,1)S(1)} all-to-all(bf16[8,64,2048]{2,1,0:T(8,128)(2,1)} %bitcast.83), channel_id=1, replica_groups=mesh['expert'=8,'tensor'=4] {'expert'}, dimensions={0} | all-to-all | bytes 4194304 | tf_op jit(solution)/shard_map/all_to_all | solution.py:134
  373.1 0.9 multiply_multiply_fusion
  (53 shorter events, 5.4 us)
Async XLA Ops:
  7.2 1.6 copy-start
  7.2 25.3 %copy-start.2 = (bf16[64,2048]{1,0:T(8,128)(2,1)S(1)}, bf16[64,2048]{1,0:T(8,128)(2,1)}, u32[]{:S(2)}) copy-start(bf16[64,2048]{1,0:T(8,128)(2,1)} %param.11) | copy-start | bytes 786436
  7.2 25.3 %copy-start.5 = (f32[2048]{0:T(1024)S(1)}, f32[2048]{0:T(1024)}, u32[]{:S(2)}) copy-start(f32[2048]{0:T(1024)} %param.12) | copy-start | bytes 24580
  7.2 25.3 %copy-start.4 = (f32[2048,64]{0,1:T(8,128)S(1)}, f32[2048,64]{0,1:T(8,128)}, u32[]{:S(2)}) copy-start(f32[2048,64]{0,1:T(8,128)} %param.13) | copy-start | bytes 1572868
  7.2 27.4 %copy-start.7 = (s32[128]{0:T(128)S(1)}, s32[128]{0:T(128)}, u32[]{:S(2)}) copy-start(s32[128]{0:T(128)} %param.15) | copy-start | bytes 1540
  11.4 18.7 %all-to-all-start = ((bf16[4,64,2048]{2,1,0:T(8,128)(2,1)}), bf16[4,64,2048]{2,1,0:T(8,128)(2,1)S(1)}, u32[]{:S(2)}, u32[]{:S(2)}) async-start(bf16[4,64,2048]{2,1,0:T(8,128)(2,1)} %bitcast), calls=%async_computation | async-start | bytes 2097152 | tf_op jit(solution)/shard_map/all_to_all | solution.py:52
  15.7 99.7 %all-gather.2.cloned.1.call-start = ((), (), s32[]{:S(2)}) async-start(), calls=%async_computation.3 | async-start | bytes 9191424 | tf_op jit(solution)/shard_map/all_gather | solution.py:74
  34.5 284.3 %reduce-scatter.2.cloned.1.call-start = ((), (), s32[]{:S(2)}) async-start(), calls=%async_computation.4 | async-start | bytes 10485760 | tf_op jit(solution)/shard_map/reduce_scatter | solution.py:128
  248.2 125.8 %copy-start.1 = (bf16[512,2048]{1,0:T(8,128)(2,1)S(1)}, bf16[512,2048]{1,0:T(8,128)(2,1)}, u32[]{:S(2)}) copy-start(bf16[512,2048]{1,0:T(8,128)(2,1)} %param.10) | copy-start | bytes 6291460
  248.3 124.9 %copy-start.6 = (f32[2048]{0:T(1024)S(1)}, f32[2048]{0:T(1024)}, u32[]{:S(2)}) copy-start(f32[2048]{0:T(1024)} %param.17) | copy-start | bytes 24580
  373.1 1.0 copy-start.3
Sparse Core Ops, SparseCore 0:
  34.6 80.6 all-gather.1
  248.4 70.3 reduce-scatter.1
where the time goes:
time: 381 us
  waiting for transfers between devices  163 us (43%)
  matrix products  116 us (30%)
  blocking collectives  53.7 us (14%)
  other arithmetic  23.2 us (6%)
  between operations  14.3 us (4%)
  local copies, waits for them, and re-layouts  6.49 us (2%)
  starting transfers between devices  4.28 us (1%)
    all_gather x1, waiting for transfers between devices, on_device(): lax.all_gather(jnp.concatenate([normed, side], axis=1), ('expert', 'tenso...  79.1 us
    reduce_scatter x1, waiting for transfers between devices, on_device(): lax.psum_scatter(combined.astype(jnp.bfloat16).reshape(-1, model_width),...  70.5 us
    all_to_all x1, blocking collectives, on_device(): lax.all_to_all(moe_sum, 'expert', split_axis=0, concat_axis=0, tiled=True)  53.7 us
    dot_general x1, matrix products, expert_inner(): jnp.einsum('nqsmd,scdf->nqsmcf', block_rows, weights[:, :2], preferred_el...  46.3 us
    dot_general x1, matrix products, on_device(): jnp.einsum('hqusr,hqsrd->qhud', pick_hot.reshape(holders, groups, row_cou...  27.4 us
    dot_general x1, matrix products, expert_down(): jnp.einsum('nqsmf,sdf->nqsmd', inner_act, weights[:, 2], preferred_elemen...  23.3 us
    all_to_all x1, waiting for transfers between devices, on_device(): lax.all_to_all(jnp.dot(context, out_proj, preferred_element_type=jnp.floa...  13.6 us
    dot_general x1, matrix products, on_device(): jnp.einsum('busr,bud->bsrd', pick_hot, all_rows, preferred_element_type=j...  13.4 us
  transfers between devices with their start and end apart: 3, of which 3 were waited for; matrix products, arithmetic and copies ran while one was open for 1% of the time, Pallas kernels for 0%

commit v1 on v0

--- a/solution.py
+++ b/solution.py
@@ -4,6 +4,30 @@
 from jax.sharding import PartitionSpec as P
 
 EPS = 1e-06
+
+
+def render_panels_up(vals, dim_i):
+    vals = jnp.moveaxis(vals, 0, dim_i)
+    v1 = vals.shape
+    return vals.reshape(*v1[:dim_i], v1[dim_i] * v1[dim_i + 1], *v1[dim_i + 2 :])
+
+
+def touch_the_ends(view, group_axis):
+    n_all = lax.axis_size(group_axis)
+    val = view[None]
+    for pp in range(n_all.bit_length() - 1):
+        e_now = 1 << pp
+        new = lax.ppermute(
+            val, axis_name=group_axis, perm=tuple(((p, p ^ e_now) for p in range(n_all)))
+        )
+        latest = jnp.stack([val, new], 0)
+        prior = lax.axis_index(group_axis) >> pp & 1
+        val = jnp.where(prior == 0, latest, latest[::-1]).reshape(-1, *view.shape)
+    return val
+
+
+def _return_all_pairs_all(local_x, matrix, dim_at):
+    return render_panels_up(touch_the_ends(local_x, matrix), dim_at)
 
 
 def rms_scale(values, gain_row):
@@ -71,8 +95,8 @@
     gate_lo = (gate_weights - gate_hi.astype(jnp.float32)).astype(jnp.bfloat16)
     side = jnp.concatenate([own_ids.astype(jnp.bfloat16), gate_hi, gate_lo], axis=1)
     side = jnp.pad(side, ((0, 0), (0, 128 - 3 * top_count)))
-    packed = lax.all_gather(
-        jnp.concatenate([normed, side], axis=1), ("expert", "tensor"), axis=0, tiled=True
+    packed = _return_all_pairs_all(
+        jnp.concatenate([normed, side], axis=1), matrix=("expert", "tensor"), dim_at=0
     ).reshape(blocks, row_count, model_width + 128)
     all_rows = packed[:, :, :model_width]
     all_ids = packed[:, :, model_width : model_width + top_count].astype(jnp.int32)

time: 381 us -> 615 us (1.61)
  waiting for transfers between devices: 163 us -> 362 us
  other arithmetic: 23.2 us -> 50.3 us
  starting transfers between devices: 4.28 us -> 11.3 us
    ppermute x0 -> x5, waiting for transfers between devices: none -> 276 us  [touch_the_ends(): lax.ppermute(val, axis_name=group_axis, perm=tuple(((p, p ^ e_now) for p...]
    all_gather x1 -> x0, waiting for transfers between devices: 79.1 us -> none  [on_device(): lax.all_gather(jnp.concatenate([normed, side], axis=1), ('expert', 'tenso...]
    select_n x0 -> x4, other arithmetic: none -> 17.8 us  [touch_the_ends(): val = jnp.where(prior == 0, latest, latest[::-1]).reshape(-1, *view.shape)]
    another operation x0 -> x7, other arithmetic: none -> 12.5 us  [touch_the_ends(): latest = jnp.stack([val, new], 0)]
    ppermute x0 -> x5, starting transfers between devices: none -> 7.11 us  [touch_the_ends(): lax.ppermute(val, axis_name=group_axis, perm=tuple(((p, p ^ e_now) for p...]
  transfers between devices with their start and end apart: 3 -> 7, of which waited for: 3 -> 7; matrix products, arithmetic and copies ran while one was open for 1% -> 0% of each run, Pallas kernels for 0% -> 0%
where the time goes in v1:
time: 615 us; the launch traced here: 614 us
  waiting for transfers between devices  362 us (59%)
  matrix products  116 us (19%)
  blocking collectives  53.9 us (9%)
  other arithmetic  50.3 us (8%)
  between operations  14.4 us (2%)
  starting transfers between devices  11.3 us (2%)
  local copies, waits for them, and re-layouts  6.5 us (1%)
    ppermute x5, waiting for transfers between devices, touch_the_ends(): lax.ppermute(val, axis_name=group_axis, perm=tuple(((p, p ^ e_now) for p...  276 us
    reduce_scatter x1, waiting for transfers between devices, on_device(): lax.psum_scatter(combined.astype(jnp.bfloat16).reshape(-1, model_width),...  71.7 us
    all_to_all x1, blocking collectives, on_device(): lax.all_to_all(moe_sum, 'expert', split_axis=0, concat_axis=0, tiled=True)  53.9 us
    dot_general x1, matrix products, expert_inner(): jnp.einsum('nqsmd,scdf->nqsmcf', block_rows, weights[:, :2], preferred_el...  46.4 us
    dot_general x1, matrix products, on_device(): jnp.einsum('hqusr,hqsrd->qhud', pick_hot.reshape(holders, groups, row_cou...  27.4 us
    dot_general x1, matrix products, expert_down(): jnp.einsum('nqsmf,sdf->nqsmd', inner_act, weights[:, 2], preferred_elemen...  23.3 us
    select_n x4, other arithmetic, touch_the_ends(): val = jnp.where(prior == 0, latest, latest[::-1]).reshape(-1, *view.shape)  17.8 us
    all_to_all x1, waiting for transfers between devices, on_device(): lax.all_to_all(jnp.dot(context, out_proj, preferred_element_type=jnp.floa...  14.3 us
  transfers between devices with their start and end apart: 7, of which 7 were waited for; matrix products, arithmetic and copies ran while one was open for 0% of the time, Pallas kernels for 0%

profile of v1, /device:TPU:0, one launch (start us, length us, event | category | flops | bytes accessed | tf_op | source)
XLA Modules:
  0.0 614.0 jit_solution(6006784594999195469)
XLA Ops:
  8.8 2.7 convolution_convert_fusion.1
  11.4 4.2 all-to-all-start
  15.8 14.3 %all-to-all-done = bf16[4,64,2048]{2,1,0:T(8,128)(2,1)S(1)} async-done(((bf16[4,64,2048]{2,1,0:T(8,128)(2,1)}), bf16[4,64,2048]{2,1,0:T(8,128)(2,1)S(1)}, u32[]{:S(2)}, u32[]{:S(2)}) %all-to-all-start) | async-done | bytes 1048608 | tf_op jit(solution)/shard_map/all_to_all | solution.py:76
  34.1 14.3 %collective-permute-done.1 = bf16[2,64,2176]{2,1,0:T(8,128)(2,1)S(1)} collective-permute-done((bf16[2,64,2176]{2,1,0:T(8,128)(2,1)S(1)}, bf16[2,64,2176]{2,1,0:T(8,128)(2,1)S(1)}, u32[]{:S(2)}, u32[]{:S(2)}) %collective-permute-start.1) | collective-permute-done | bytes 557088 | tf_op jit(solution)/shard_map/ppermute | solution.py:20
  48.7 2.3 collective-permute-start.2
  51.0 24.1 %collective-permute-done.2 = bf16[4,64,2176]{2,1,0:T(8,128)(2,1)} collective-permute-done((bf16[4,64,2176]{2,1,0:T(8,128)(2,1)S(1)}, bf16[4,64,2176]{2,1,0:T(8,128)(2,1)}, u32[]{:S(2)}, u32[]{:S(2)}) %collective-permute-start.2) | collective-permute-done | bytes 1114144 | tf_op jit(solution)/shard_map/ppermute | solution.py:20
  76.6 1.9 reverse_select_fusion.2
  78.5 1.8 collective-permute-start.3
  80.3 47.5 %collective-permute-done.3 = bf16[8,64,2176]{2,1,0:T(8,128)(2,1)} collective-permute-done((bf16[8,64,2176]{2,1,0:T(8,128)(2,1)}, bf16[8,64,2176]{2,1,0:T(8,128)(2,1)}, u32[]{:S(2)}, u32[]{:S(2)}) %collective-permute-start.3) | collective-permute-done | bytes 2228256 | tf_op jit(solution)/shard_map/ppermute | solution.py:20
  127.8 2.7 pad_maximum_fusion.1
  130.6 3.1 reverse_select_fusion.1
  133.7 2.5 collective-permute-start.4
  137.8 188.4 %collective-permute-done.4 = bf16[16,64,2176]{2,1,0:T(8,128)(2,1)} collective-permute-done((bf16[16,64,2176]{2,1,0:T(8,128)(2,1)}, bf16[16,64,2176]{2,1,0:T(8,128)(2,1)}, u32[]{:S(2)}, u32[]{:S(2)}) %collective-permute-start.4) | collective-permute-done | bytes 4456480 | tf_op jit(solution)/shard_map/ppermute | solution.py:20
  326.2 7.9 %pad_maximum_fusion = bf16[2,16,64,2176]{3,2,1,0:T(8,128)(2,1)} fusion(bf16[1,16,64,2176]{3,2,1,0:T(8,128)(2,1)} %bitcast.15, bf16[1,16,64,2176]{3,2,1,0:T(8,128)(2,1)} %bitcast.13), kind=kLoop, calls=%fused_computation.13 | loop fusion | flops 4456448 | bytes 17825792 | tf_op jit(solution)/shard_map/stack | solution.py:23
  334.2 12.7 %reverse_select_fusion = bf16[2,16,64,2176]{3,2,1,0:T(8,128)(2,1)} fusion(bf16[2,16,64,2176]{3,2,1,0:T(8,128)(2,1)} %pad_maximum_fusion, pred[]{:T(512)S(6)} %eq.122), kind=kLoop, calls=%fused_computation.12 | loop fusion | flops 4456448 | bytes 17825792 | tf_op jit(solution)/shard_map/jit(_where)/select_n | solution.py:25
  346.8 2.1 fusion.71
  349.0 3.7 fusion.18
  353.7 8.8 %fusion.21 = (bf16[32,64,64]{2,1,0:T(8,128)(2,1)}, bf16[32,64,64]{2,1,0:T(8,128)(2,1)S(1)}) fusion(s32[32,64,8]{2,1,0:T(8,128)S(1)} %get-tuple-element.10, bf16[32,64,8]{2,1,0:T(8,128)(2,1)S(1)} %get-tuple-element.9, bf16[32,64,8]{2,1,0:T(8,128)(2,1)S(1)} %get-tuple-element.8), kind=kLoop, calls=%fused_computation.27 | loop fusion | flops 4980736 | bytes 655360 | tf_op jit(solution)/shard_map/reduce_sum | solution.py:118
  368.2 13.4 %convolution_convert_fusion = bf16[32,16,10,2048]{3,1,2,0:T(8,128)(2,1)} fusion(bf16[32,64,2176]{2,1,0:T(8,128)(2,1)} %bitcast.96, f32[32,64,16]{1,2,0:T(8,128)S(1)} %get-tuple-element.14, f32[32,64,16]{1,2,0:T(8,128)S(1)} %copy.61), kind=kOutput, calls=%fused_computation.11 | convolution fusion | flops 1353318400 | bytes 29622272 | tf_op jit(solution)/shard_map/busr,bud->bsrd/dot_general | solution.py:134
  382.8 46.4 %fusion.8 = f32[8,4,16,10,2,256]{5,3,4,1,0,2:T(8,128)} fusion(bf16[16,3,2048,256]{3,2,1,0:T(8,128)(2,1)} %param.16, bf16[8,4,16,10,2048,1]{4,2,3,1,0,5:T(8,128)(2,1)} %bitcast.97), kind=kOutput, calls=%fused_computation.14 | convolution fusion | flops 10737418240 | bytes 65011712 | tf_op jit(solution)/shard_map/nqsmd,scdf->nqsmcf/dot_general | solution.py:39
  429.2 23.3 %convert_bitcast_fusion = bf16[8,4,16,10,2048]{4,3,1,0,2:T(8,128)(2,1)} fusion(bf16[16,3,2048,256]{3,2,1,0:T(8,128)(2,1)} %param.16, f32[8,4,16,10,2,256]{5,3,4,1,0,2:T(8,128)} %fusion.8, f32[8,4,16,10]{3,1,0,2:T(4,128)S(1)} %copy.64), kind=kOutput, calls=%fused_computation.4 | convolution fusion | flops 5388369920 | bytes 54546432 | tf_op jit(solution)/shard_map/nqsmf,sdf->nqsmd/dot_general | solution.py:46
  452.5 27.4 %bitcast_convert_fusion = bf16[4,8,64,2048]{3,2,1,0:T(8,128)(2,1)} fusion(bf16[8,4,16,10,2048]{4,3,1,0,2:T(8,128)(2,1)} %convert_bitcast_fusion, f32[8,4,64,16]{2,3,0,1:T(8,128)S(1)} %copy.59, f32[8,4,64,16]{2,3,1,0:T(8,128)S(1)} %bitcast.101), kind=kOutput, calls=%fused_computation.9 | convolution fusion | flops 1347026944 | bytes 29622272 | tf_op jit(solution)/shard_map/hqusr,hqsrd->qhud/dot_general | solution.py:146
  480.0 71.7 %reduce-scatter.2.cloned.1.call-done = bf16[512,2048]{1,0:T(8,128)(2,1)} async-done(((bf16[2048,2048]{1,0:T(8,128)(2,1)}), bf16[512,2048]{1,0:T(8,128)(2,1)}) %reduce-scatter.2.cloned.1.call-update) | async-done | bytes 2097168 | tf_op jit(solution)/shard_map/reduce_scatter | solution.py:152
  551.7 53.9 %all_to_all.10 = bf16[8,64,2048]{2,1,0:T(8,128)(2,1)S(1)} all-to-all(bf16[8,64,2048]{2,1,0:T(8,128)(2,1)} %bitcast.104), channel_id=1, replica_groups=mesh['expert'=8,'tensor'=4] {'expert'}, dimensions={0} | all-to-all | bytes 4194304 | tf_op jit(solution)/shard_map/all_to_all | solution.py:158
  (72 shorter events, 18.4 us)
Async XLA Ops:
  7.2 1.6 copy-start
  7.2 8.5 %copy-start.7 = (s32[256,8]{0,1:T(8,128)S(1)}, s32[256,8]{0,1:T(8,128)}, u32[]{:S(2)}) copy-start(s32[256,8]{0,1:T(8,128)} %param.14) | copy-start | bytes 24580
  7.2 23.1 %copy-start.2 = (bf16[64,2048]{1,0:T(8,128)(2,1)S(1)}, bf16[64,2048]{1,0:T(8,128)(2,1)}, u32[]{:S(2)}) copy-start(bf16[64,2048]{1,0:T(8,128)(2,1)} %param.11) | copy-start | bytes 786436
  7.2 23.3 %copy-start.5 = (f32[2048]{0:T(1024)S(1)}, f32[2048]{0:T(1024)}, u32[]{:S(2)}) copy-start(f32[2048]{0:T(1024)} %param.12) | copy-start | bytes 24580
  7.2 23.4 %copy-start.4 = (f32[2048,64]{0,1:T(8,128)S(1)}, f32[2048,64]{0,1:T(8,128)}, u32[]{:S(2)}) copy-start(f32[2048,64]{0,1:T(8,128)} %param.13) | copy-start | bytes 1572868
  11.4 18.7 %all-to-all-start = ((bf16[4,64,2048]{2,1,0:T(8,128)(2,1)}), bf16[4,64,2048]{2,1,0:T(8,128)(2,1)S(1)}, u32[]{:S(2)}, u32[]{:S(2)}) async-start(bf16[4,64,2048]{2,1,0:T(8,128)(2,1)} %bitcast), calls=%async_computation | async-start | bytes 2097152 | tf_op jit(solution)/shard_map/all_to_all | solution.py:76
  15.7 536.0 %reduce-scatter.2.cloned.1.call-start = ((), (), s32[]{:S(2)}) async-start(), calls=%async_computation.3 | async-start | bytes 10485760 | tf_op jit(solution)/shard_map/reduce_scatter | solution.py:152
  31.9 1.6 collective-permute-start
  33.7 14.7 %collective-permute-start.1 = (bf16[2,64,2176]{2,1,0:T(8,128)(2,1)S(1)}, bf16[2,64,2176]{2,1,0:T(8,128)(2,1)S(1)}, u32[]{:S(2)}, u32[]{:S(2)}) collective-permute-start(bf16[2,64,2176]{2,1,0:T(8,128)(2,1)S(1)} %get-tuple-element.12), channel_id=1, source_target_pairs={{0,2},{1,3},{2,0},{3,1},{4,6},{5,7},{6,4},{7,5},{8,10},{9,11},{10,... | collective-permute-start | bytes 1671176 | tf_op jit(solution)/shard_map/ppermute | solution.py:20
  48.7 26.4 %collective-permute-start.2 = (bf16[4,64,2176]{2,1,0:T(8,128)(2,1)S(1)}, bf16[4,64,2176]{2,1,0:T(8,128)(2,1)}, u32[]{:S(2)}, u32[]{:S(2)}) collective-permute-start(bf16[4,64,2176]{2,1,0:T(8,128)(2,1)S(1)} %bitcast.99), channel_id=1, source_target_pairs={{0,4},{1,5},{2,6},{3,7},{4,0},{5,1},{6,2},{7,3},{8,12},{9,13},{10,... | collective-permute-start | bytes 3342344 | tf_op jit(solution)/shard_map/ppermute | solution.py:20
  78.5 49.3 %collective-permute-start.3 = (bf16[8,64,2176]{2,1,0:T(8,128)(2,1)}, bf16[8,64,2176]{2,1,0:T(8,128)(2,1)}, u32[]{:S(2)}, u32[]{:S(2)}) collective-permute-start(bf16[8,64,2176]{2,1,0:T(8,128)(2,1)} %bitcast.11), channel_id=1, source_target_pairs={{0,8},{1,9},{2,10},{3,11},{4,12},{5,13},{6,14},{7,15},{8,0},{9,1},... | collective-permute-start | bytes 6684680 | tf_op jit(solution)/shard_map/ppermute | solution.py:20
  130.5 5.7 copy-start.8
  133.7 192.6 %collective-permute-start.4 = (bf16[16,64,2176]{2,1,0:T(8,128)(2,1)}, bf16[16,64,2176]{2,1,0:T(8,128)(2,1)}, u32[]{:S(2)}, u32[]{:S(2)}) collective-permute-start(bf16[16,64,2176]{2,1,0:T(8,128)(2,1)} %bitcast.14), channel_id=1, source_target_pairs={{0,16},{1,17},{2,18},{3,19},{4,20},{5,21},{6,22},{7,23},{8,24},{9,... | collective-permute-start | bytes 13369352 | tf_op jit(solution)/shard_map/ppermute | solution.py:20
  480.0 126.2 %copy-start.6 = (f32[2048]{0:T(1024)S(1)}, f32[2048]{0:T(1024)}, u32[]{:S(2)}) copy-start(f32[2048]{0:T(1024)} %param.17) | copy-start | bytes 24580
  551.7 55.4 %copy-start.1 = (bf16[512,2048]{1,0:T(8,128)(2,1)S(1)}, bf16[512,2048]{1,0:T(8,128)(2,1)}, u32[]{:S(2)}) copy-start(bf16[512,2048]{1,0:T(8,128)(2,1)} %param.10) | copy-start | bytes 6291460
  606.2 1.0 copy-start.3
Sparse Core Ops, SparseCore 0:
  480.1 71.5 reduce-scatter.1
